TPU v7x, 256 devices: a whole 4x4x8 slice. The times are simulated.
256 devices in a mesh: in: 4 (over x), out: 64 (over z, y, core).
Axes of the slice: x: 4, y: 4, z: 8, core: 2. Of those that a mesh axis runs over, the one named last changes fastest.
Arguments:
- activations: bfloat16 [8192, 4096], P('out', 'in'), may hold values from -6 to 6
- out_grad: bfloat16 [8192, 16384], P('in', 'out'), may hold values from -0.06591797 to 0.06591797
- block_rows: int32 [4, 64, 4], P('in', 'out'), may hold values from 0 to 31, as said below
- block_cols: int32 [4, 64, 4], P('in', 'out'), may hold values from 0 to 127, as said below
- counts: int32 [4, 64], P('in', 'out'), may hold values from 1 to 4, as said below
Outputs:
- grad_blocks: float32 [4, 64, 4, 128, 128], P('in', 'out')
Inputs may be any that keep to these rules, and one draw needn't show every extreme that they name: `block_rows`: tile (i, j) lists blocks of its own region only: rows i * 8 to (i + 1) * 8 - 1; slots of one tile name different blocks, and slots past counts[i, j] also name blocks of the tile. `block_cols`: columns j * 2 to (j + 1) * 2 - 1 for tile (i, j). `counts`: some tile has a full list in every draw.
All inputs are finite; a program needn't handle non-finite values.
Results may differ from a plain program's by a relative error of at most 0.0003.
Values may be sent and summed in bfloat16 or wider, within the bound.
No kernel may reach another device: no remote copies, remote signals or barrier semaphores. Data moves between devices by JAX's collectives and lax.ppermute only.
A program may use at most 128 MiB of HBM per device.

v0:
```python
import jax
import jax.numpy as jnp
from jax import lax
from jax.sharding import PartitionSpec as P

BLK = 128
MAXB = 4


def block_products(left_rows, grad_rows, local_cols, tile_cols):
    width = grad_rows.shape[0]
    right = jnp.take(grad_rows.reshape(width, tile_cols, BLK), local_cols, axis=1)
    return jnp.einsum("nbi,nbj->bij", left_rows, right, preferred_element_type=jnp.float32)


def on_device(activations, out_grad, block_rows, block_cols, counts):
    in_place = lax.axis_index("in")
    out_place = lax.axis_index("out")
    tile_rows = activations.shape[1] // BLK
    tile_cols = out_grad.shape[1] // BLK
    local_rows = block_rows[0, 0] - in_place * tile_rows
    local_cols = block_cols[0, 0] - out_place * tile_cols
    live = counts[0, 0]
    grad_all = lax.all_gather(out_grad, "in", axis=0, tiled=True)
    piece = lax.all_gather(activations, "out", axis=0, tiled=True)
    height = piece.shape[0]
    left = jnp.take(piece.reshape(height, tile_rows, BLK), local_rows, axis=1)
    totals = block_products(left, grad_all, local_cols, tile_cols)
    keep = (jnp.arange(MAXB, dtype=jnp.int32) < live)[:, None, None]
    result = jnp.where(keep, totals, jnp.zeros_like(totals))
    return result.reshape(1, 1, MAXB, BLK, BLK)


def solution(mesh):
    return jax.shard_map(
        on_device,
        mesh=mesh,
        in_specs=(
            P("out", "in"),
            P("in", "out"),
            P("in", "out", None),
            P("in", "out", None),
            P("in", "out"),
        ),
        out_specs=P("in", "out", None, None, None),
        check_vma=False,
    )
```

profile of v0, /device:TPU:1, one launch (start us, length us, event | category | flops | bytes accessed | tf_op | source)
XLA Modules:
  0.0 228.5 jit_solution(16223086437838721816)
XLA Ops:
  6.5 0.0 all-gather.5.cloned.1.call-start
  6.5 0.7 all-gather.5.cloned.1.call-update
  7.3 0.0 all-gather.3.cloned.1.call-start
  7.3 0.7 all-gather.3.cloned.1.call-update
  8.7 0.7 fusion.11
  9.3 0.7 fusion.10
  10.0 0.7 compare_and_fusion
  10.7 52.8 %all-gather.5.cloned.1.call-done = bf16[8192,256]{1,0:T(8,128)(2,1)} async-done(((bf16[2048,256]{1,0:T(8,128)(2,1)}), bf16[8192,256]{1,0:T(8,128)(2,1)}) %all-gather.5.cloned.1.call-update) | async-done | bytes 4194320 | tf_op jit(solution)/shard_map/all_gather | solution.py:24
  63.5 4.5 %fusion.15 = (bf16[4096,256]{1,0:T(8,128)(2,1)}, bf16[4096,256]{1,0:T(8,128)(2,1)}) fusion(bf16[8192,256]{1,0:T(8,128)(2,1)} %all-gather.5.cloned.1.call-done), kind=kLoop, calls=%fused_computation.30 | loop fusion | bytes 8388608 | tf_op jit(solution)/shard_map/jit(_take)/gather | solution.py:12
  68.0 2.9 %copy.9 = bf16[4096,256]{0,1:T(8,128)(2,1)S(1)} copy(bf16[4096,256]{1,0:T(8,128)(2,1)} %get-tuple-element.7) | data formatting | bytes 4194304 | tf_op jit(solution)/shard_map/jit(_take)/gather | solution.py:12
  70.9 4.1 %copy.10 = bf16[4096,256]{0,1:T(8,128)(2,1)} copy(bf16[4096,256]{1,0:T(8,128)(2,1)} %get-tuple-element.8) | data formatting | bytes 4194304 | tf_op jit(solution)/shard_map/jit(_take)/gather | solution.py:12
  75.0 2.8 %gather_fusion.2 = bf16[4,4096,128]{1,2,0:T(8,128)(2,1)} fusion(bf16[4096,2,128]{0,2,1:T(8,128)(2,1)S(1)} %bitcast.26, s32[1024]{0:T(1024)S(1)} %pad_clamp_fusion), kind=kCustom, calls=%fused_computation.2 | custom fusion | bytes 8388624 | tf_op jit(solution)/shard_map/jit(_take)/gather | solution.py:12
  77.8 4.6 %gather_fusion.3 = bf16[4,4096,128]{1,2,0:T(8,128)(2,1)} fusion(bf16[4096,2,128]{0,2,1:T(8,128)(2,1)} %bitcast.27, s32[1024]{0:T(1024)S(1)} %pad_clamp_fusion), kind=kCustom, calls=%fused_computation.3 | custom fusion | bytes 8388624 | tf_op jit(solution)/shard_map/jit(_take)/gather | solution.py:12
  82.4 84.2 %all-gather.3.cloned.1.call-done = bf16[8192,1024]{1,0:T(8,128)(2,1)} async-done(((bf16[128,1024]{1,0:T(8,128)(2,1)}), bf16[8192,1024]{1,0:T(8,128)(2,1)}) %all-gather.3.cloned.1.call-update) | async-done | bytes 16777232 | tf_op jit(solution)/shard_map/all_gather | solution.py:25
  166.5 11.6 %fusion.14 = (bf16[4096,1024]{1,0:T(8,128)(2,1)}, bf16[4096,1024]{1,0:T(8,128)(2,1)}) fusion(bf16[8192,1024]{1,0:T(8,128)(2,1)} %all-gather.3.cloned.1.call-done), kind=kLoop, calls=%fused_computation.29 | loop fusion | bytes 33554432 | tf_op jit(solution)/shard_map/jit(_take)/gather | solution.py:27
  178.2 11.3 %copy.7 = bf16[4096,1024]{0,1:T(8,128)(2,1)} copy(bf16[4096,1024]{1,0:T(8,128)(2,1)} %get-tuple-element.5) | data formatting | bytes 16777216 | tf_op jit(solution)/shard_map/jit(_take)/gather | solution.py:27
  189.5 11.8 %copy.8 = bf16[4096,1024]{0,1:T(8,128)(2,1)} copy(bf16[4096,1024]{1,0:T(8,128)(2,1)} %get-tuple-element.6) | data formatting | bytes 16777216 | tf_op jit(solution)/shard_map/jit(_take)/gather | solution.py:27
  201.3 6.1 %gather_fusion = bf16[4,4096,128]{1,2,0:T(8,128)(2,1)} fusion(bf16[4096,8,128]{0,2,1:T(8,128)(2,1)} %bitcast.24, s32[1024]{0:T(1024)S(1)} %pad_clamp_fusion.1), kind=kCustom, calls=%fused_computation | custom fusion | bytes 8388624 | tf_op jit(solution)/shard_map/jit(_take)/gather | solution.py:27
  207.4 6.2 %gather_fusion.1 = bf16[4,4096,128]{1,2,0:T(8,128)(2,1)} fusion(bf16[4096,8,128]{0,2,1:T(8,128)(2,1)} %bitcast.25, s32[1024]{0:T(1024)S(1)} %pad_clamp_fusion.1), kind=kCustom, calls=%fused_computation.1 | custom fusion | bytes 8388624 | tf_op jit(solution)/shard_map/jit(_take)/gather | solution.py:27
  213.6 8.1 %fusion.9 = f32[1,1,4,128,128]{4,3,2,1,0:T(8,128)} fusion(bf16[4096,4,128]{0,2,1:T(8,128)(2,1)} %bitcast.29, bf16[4096,4,128]{0,2,1:T(8,128)(2,1)} %bitcast.28, pred[4]{0:T(512)(128)(4,1)S(1)} %get-tuple-element.9, bf16[4096,4,128]{0,2,1:T(8,128)(2,1)} %bitcast.31, bf16[4096,4,128]{0,2,1:T(8,128)(2,1)} %bitcast.30, pred[4]{0:T(512)(128)(4,1)S(1)} %get-tuple-element.10, ...), kind=kOutput, calls=%fused_computation.15 | convolution fusion | flops 1115750400 | bytes 17039372 | tf_op jit(solution)/shard_map/nbi,nbj->bij/dot_general | solution.py:13
  (3 shorter events, 0.0 us)
Async XLA Ops:
  6.5 57.0 %all-gather.5.cloned.1.call-start = ((), (), s32[]{:S(2)}) async-start(), calls=%async_computation.1 | async-start | bytes 5242880 | tf_op jit(solution)/shard_map/all_gather | solution.py:24
  7.3 159.3 %all-gather.3.cloned.1.call-start = ((), (), s32[]{:S(2)}) async-start(), calls=%async_computation | async-start | bytes 17039360 | tf_op jit(solution)/shard_map/all_gather | solution.py:25
Sparse Core Ops, SparseCore 0:
  9.1 54.3 all-gather.4
  66.3 100.2 all-gather.2
where the time goes:
time: 229 us
  waiting for transfers between devices  138 us (60%)
  local copies, waits for them, and re-layouts  65.8 us (29%)
  between operations  14.1 us (6%)
  matrix products  8.1 us (4%)
    all_gather x1, waiting for transfers between devices, on_device(): piece = lax.all_gather(activations, 'out', axis=0, tiled=True)  84.2 us
    all_gather x1, waiting for transfers between devices, on_device(): grad_all = lax.all_gather(out_grad, 'in', axis=0, tiled=True)  52.8 us
    gather x5, local copies, waits for them, and re-layouts, on_device(): left = jnp.take(piece.reshape(height, tile_rows, BLK), local_rows, axis=1)  47 us
    gather x5, local copies, waits for them, and re-layouts, block_products(): jnp.take(grad_rows.reshape(width, tile_cols, BLK), local_cols, axis=1)  18.8 us
    dot_general x1, matrix products, block_products(): jnp.einsum('nbi,nbj->bij', left_rows, right, preferred_element_type=jnp.f...  8.1 us
  transfers between devices with their start and end apart: 2, of which 2 were waited for; matrix products, arithmetic and copies ran while one was open for 9% of the time, Pallas kernels for 0%

commit v1 on v0

--- a/solution.py
+++ b/solution.py
@@ -22,7 +22,9 @@
     local_cols = block_cols[0, 0] - out_place * tile_cols
     live = counts[0, 0]
     grad_all = lax.all_gather(out_grad, "in", axis=0, tiled=True)
-    piece = lax.all_gather(activations, "out", axis=0, tiled=True)
+    piece = jnp.concatenate(
+        lax.all_to_all(jnp.stack([activations] * lax.axis_size("out")), "out", 0, 0), axis=0
+    )
     height = piece.shape[0]
     left = jnp.take(piece.reshape(height, tile_rows, BLK), local_rows, axis=1)
     totals = block_products(left, grad_all, local_cols, tile_cols)

time: 229 us -> 488 us (2.13); the launches traced: 229 us -> 479 us
  waiting for transfers between devices: 138 us -> 343 us
  local copies, waits for them, and re-layouts: 65.8 us -> 100 us
  starting transfers between devices: 0.04 us -> 13.5 us
    all_to_all x0 -> x1, waiting for transfers between devices: none -> 290 us  [on_device(): lax.all_to_all(jnp.stack([activations] * lax.axis_size('out')), 'out', 0, 0)]
    all_gather x1 -> x0, waiting for transfers between devices: 84.2 us -> none  [on_device(): piece = lax.all_gather(activations, 'out', axis=0, tiled=True)]
    gather x5 -> x7, local copies, waits for them, and re-layouts: 47 us -> 74.4 us  [on_device(): left = jnp.take(piece.reshape(height, tile_rows, BLK), local_rows, axis=1)]
    all_to_all x0 -> x1, starting transfers between devices: none -> 13.5 us  [on_device(): lax.all_to_all(jnp.stack([activations] * lax.axis_size('out')), 'out', 0, 0)]
    another operation x0 -> x1, local copies, waits for them, and re-layouts: none -> 6.2 us  [on_device(): jnp.stack([activations] * lax.axis_size('out'))]
  transfers between devices with their start and end apart: 2 -> 2, of which waited for: 2 -> 2; matrix products, arithmetic and copies ran while one was open for 9% -> 4% of each run, Pallas kernels for 0% -> 0%
where the time goes in v1:
time: 488 us; the launch traced here: 479 us
  waiting for transfers between devices  343 us (70%)
  local copies, waits for them, and re-layouts  100 us (20%)
  between operations  14.1 us (3%)
  starting transfers between devices  13.5 us (3%)
  matrix products  8.1 us (2%)
    all_to_all x1, waiting for transfers between devices, on_device(): lax.all_to_all(jnp.stack([activations] * lax.axis_size('out')), 'out', 0, 0)  290 us
    gather x7, local copies, waits for them, and re-layouts, on_device(): left = jnp.take(piece.reshape(height, tile_rows, BLK), local_rows, axis=1)  74.4 us
    all_gather x1, waiting for transfers between devices, on_device(): grad_all = lax.all_gather(out_grad, 'in', axis=0, tiled=True)  52.7 us
    gather x5, local copies, waits for them, and re-layouts, block_products(): jnp.take(grad_rows.reshape(width, tile_cols, BLK), local_cols, axis=1)  18.7 us
    all_to_all x1, starting transfers between devices, on_device(): lax.all_to_all(jnp.stack([activations] * lax.axis_size('out')), 'out', 0, 0)  13.5 us
  transfers between devices with their start and end apart: 2, of which 2 were waited for; matrix products, arithmetic and copies ran while one was open for 4% of the time, Pallas kernels for 0%

profile of v1, /device:TPU:1, one launch (start us, length us, event | category | flops | bytes accessed | tf_op | source)
XLA Modules:
  0.0 479.3 jit_solution(12984525636216984914)
XLA Ops:
  6.5 1.1 copy.11
  7.7 6.2 %stack.2 = bf16[64,128,1024]{1,2,0:T(8,128)(2,1)} broadcast(bf16[128,1024]{0,1:T(8,128)(2,1)S(1)} %copy.11), dimensions={1,2} | broadcast | bytes 17039360 | tf_op jit(solution)/shard_map/stack | solution.py:26
  13.9 0.0 copy-start.1
  13.9 0.0 copy-start
  13.9 13.5 %all-to-all-start = ((bf16[64,128,1024]{1,2,0:T(8,128)(2,1)}), bf16[64,128,1024]{1,2,0:T(8,128)(2,1)}, u32[]{:S(2)}, u32[]{:S(2)}) async-start(bf16[64,128,1024]{1,2,0:T(8,128)(2,1)} %stack.2), calls=%async_computation | async-start | bytes 33554432 | tf_op jit(solution)/shard_map/all_to_all | solution.py:26
  27.3 0.0 all-gather.2.cloned.1.call-start
  27.4 0.7 all-gather.2.cloned.1.call-update
  28.7 0.0 copy-done.1
  28.8 0.0 copy-done
  28.8 52.7 %all-gather.2.cloned.1.call-done = bf16[8192,256]{1,0:T(8,128)(2,1)} async-done(((bf16[2048,256]{1,0:T(8,128)(2,1)}), bf16[8192,256]{1,0:T(8,128)(2,1)}) %all-gather.2.cloned.1.call-update) | async-done | bytes 4194320 | tf_op jit(solution)/shard_map/all_gather | solution.py:24
  81.5 4.4 fusion.15
  85.9 2.9 copy.14
  88.8 4.1 copy.15
  92.9 2.8 gather_fusion.2
  95.7 4.5 gather_fusion.3
  100.2 289.7 %all-to-all-done = bf16[64,128,1024]{1,2,0:T(8,128)(2,1)} async-done(((bf16[64,128,1024]{1,2,0:T(8,128)(2,1)}), bf16[64,128,1024]{1,2,0:T(8,128)(2,1)}, u32[]{:S(2)}, u32[]{:S(2)}) %all-to-all-start) | async-done | bytes 16777248 | tf_op jit(solution)/shard_map/all_to_all | solution.py:26
  389.9 11.5 %fusion.14 = (bf16[32,128,1024]{1,2,0:T(8,128)(2,1)}, bf16[32,128,1024]{1,2,0:T(8,128)(2,1)}) fusion(bf16[64,128,1024]{1,2,0:T(8,128)(2,1)} %all-to-all-done), kind=kLoop, calls=%fused_computation.29 | loop fusion | bytes 33554432 | tf_op jit(solution)/shard_map/jit(_take)/gather | solution.py:29
  401.4 12.0 %copy.12 = bf16[32,128,1024]{1,0,2:T(8,128)(2,1)} copy(bf16[32,128,1024]{1,2,0:T(8,128)(2,1)} %get-tuple-element.5) | data formatting | bytes 16777216 | tf_op jit(solution)/shard_map/jit(_take)/gather | solution.py:29
  413.4 13.3 %reshape.72 = bf16[4096,8,128]{0,2,1:T(8,128)(2,1)} reshape(bf16[32,128,1024]{1,0,2:T(8,128)(2,1)} %copy.12) | data formatting | bytes 16777216 | tf_op jit(solution)/shard_map/jit(_take)/gather | solution.py:29
  426.7 12.0 %copy.13 = bf16[32,128,1024]{1,0,2:T(8,128)(2,1)} copy(bf16[32,128,1024]{1,2,0:T(8,128)(2,1)} %get-tuple-element.6) | data formatting | bytes 16777216 | tf_op jit(solution)/shard_map/jit(_take)/gather | solution.py:29
  438.7 13.3 %reshape.73 = bf16[4096,8,128]{0,2,1:T(8,128)(2,1)} reshape(bf16[32,128,1024]{1,0,2:T(8,128)(2,1)} %copy.13) | data formatting | bytes 16777216 | tf_op jit(solution)/shard_map/jit(_take)/gather | solution.py:29
  452.0 6.1 %gather_fusion = bf16[4,4096,128]{1,2,0:T(8,128)(2,1)} fusion(bf16[4096,8,128]{0,2,1:T(8,128)(2,1)} %reshape.72, s32[1024]{0:T(1024)S(1)} %pad_clamp_fusion.1), kind=kCustom, calls=%fused_computation | custom fusion | bytes 8388624 | tf_op jit(solution)/shard_map/jit(_take)/gather | solution.py:29
  458.2 6.1 %gather_fusion.1 = bf16[4,4096,128]{1,2,0:T(8,128)(2,1)} fusion(bf16[4096,8,128]{0,2,1:T(8,128)(2,1)} %reshape.73, s32[1024]{0:T(1024)S(1)} %pad_clamp_fusion.1), kind=kCustom, calls=%fused_computation.1 | custom fusion | bytes 8388624 | tf_op jit(solution)/shard_map/jit(_take)/gather | solution.py:29
  464.3 8.1 %fusion.9 = f32[1,1,4,128,128]{4,3,2,1,0:T(8,128)} fusion(bf16[4096,4,128]{0,2,1:T(8,128)(2,1)} %bitcast.29, bf16[4096,4,128]{0,2,1:T(8,128)(2,1)} %bitcast.28, pred[4]{0:T(512)(128)(4,1)S(1)} %get-tuple-element.9, bf16[4096,4,128]{0,2,1:T(8,128)(2,1)} %bitcast.31, bf16[4096,4,128]{0,2,1:T(8,128)(2,1)} %bitcast.30, pred[4]{0:T(512)(128)(4,1)S(1)} %get-tuple-element.10, ...), kind=kOutput, calls=%fused_computation.15 | convolution fusion | flops 1115750400 | bytes 17039372 | tf_op jit(solution)/shard_map/nbi,nbj->bij/dot_general | solution.py:13
  (6 shorter events, 0.0 us)
Async XLA Ops:
  13.9 14.9 %copy-start.1 = (s32[1,1,4]{2,1,0:T(1,128)S(1)}, s32[1,1,4]{2,1,0:T(1,128)}, u32[]{:S(2)}) copy-start(s32[1,1,4]{2,1,0:T(1,128)} %param.7) | copy-start | bytes 52
  13.9 14.9 %copy-start = (s32[1,1,4]{2,1,0:T(1,128)S(1)}, s32[1,1,4]{2,1,0:T(1,128)}, u32[]{:S(2)}) copy-start(s32[1,1,4]{2,1,0:T(1,128)} %param.8) | copy-start | bytes 52
  13.9 376.0 %all-to-all-start = ((bf16[64,128,1024]{1,2,0:T(8,128)(2,1)}), bf16[64,128,1024]{1,2,0:T(8,128)(2,1)}, u32[]{:S(2)}, u32[]{:S(2)}) async-start(bf16[64,128,1024]{1,2,0:T(8,128)(2,1)} %stack.2), calls=%async_computation | async-start | bytes 33554432 | tf_op jit(solution)/shard_map/all_to_all | solution.py:26
  27.3 54.2 %all-gather.2.cloned.1.call-start = ((), (), s32[]{:S(2)}) async-start(), calls=%async_computation.1 | async-start | bytes 5242880 | tf_op jit(solution)/shard_map/all_gather | solution.py:24
Sparse Core Ops, SparseCore 0:
  30.0 51.4 all-gather.1
